TPU v7x, 512 devices: a whole 4x4x16 slice. The times are simulated.
512 devices in a mesh: seq: 32 (over z_lo, y), tensor: 8 (over z_hi, x), enc: 2 (over core).
Axes of the slice: x: 4, y: 4, z: 16 (z_hi: 2, z_lo: 8; z = z_hi * 8 + z_lo), core: 2. Of those that a mesh axis runs over, the one named last changes fastest.
Arguments:
- neighbour_rows: bfloat16 [32768, 1024], P('seq'), may hold values from -17 to 17
- norm_gain: float32 [1024], replicated, may hold values from 0.1 to 1.9
- up_weight: bfloat16 [1024, 4096], P(None, ('tensor', 'enc')), may hold values from -0.1875 to 0.1875
- down_weight: bfloat16 [4096, 1024], P(('tensor', 'enc')), may hold values from -0.09375 to 0.09375
- final_gain: float32 [1024], replicated, may hold values from 0.1 to 1.9
- key_weight: bfloat16 [1024, 4096], P(None, ('tensor', 'enc')), may hold values from -0.1875 to 0.1875
- value_weight: bfloat16 [1024, 4096], P(None, ('tensor', 'enc')), may hold values from -0.1875 to 0.1875
- queries: bfloat16 [32768, 4096], P('seq', ('tensor', 'enc')), may hold values from -170 to 170
- block_lists: int32 [512, 2], P('seq'), may hold values from 0 to 255, as said below
- live_counts: int32 [512], P('seq'), may hold values from 1 to 2
Outputs:
- attended: bfloat16 [32768, 4096], P('seq', ('tensor', 'enc'))
Inputs may be any that keep to these rules, and one draw needn't show every extreme that they name: `block_lists`: block b of the pool lies on the device of index b // 8 along seq. The two entries of a span name blocks of two different devices. Among all list entries of one device's spans (those beyond a span's count included) at most 1 name blocks of any one device, and in every draw some device's entries reach 1 for some device.
All inputs are finite; a program needn't handle non-finite values.
Results may differ from a plain program's by a relative error of at most 0.019.
The roundings to bfloat16 on the way count: a program that leaves them out, or rounds other values in their place, can miss the bound.
Values may be sent and summed in bfloat16 or wider, within the bound.
No kernel may reach another device: no remote copies, remote signals or barrier semaphores. Data moves between devices by JAX's collectives and lax.ppermute only.
A program may use at most 64 MiB of HBM per device.

v0:
```python
import math

import jax
import jax.numpy as jnp
from jax import lax
from jax.sharding import PartitionSpec as P

DH = 128
NB = 128
CL = 64
KMAX = 2


def rms_scale(rows, gain):
    mean_square = jnp.mean(rows * rows, axis=-1, keepdims=True)
    return rows * lax.rsqrt(mean_square + 1e-06) * gain


def need_ranks(owners):
    need_count = owners.shape[-1]
    order_index = jnp.arange(need_count)
    same_owner = owners[..., :, None] == owners[..., None, :]
    earlier = order_index[None, :] < order_index[:, None]
    return jnp.sum(jnp.logical_and(same_owner, earlier), axis=-1)


def shards(
    neighbour_rows,
    norm_gain,
    up_weight,
    down_weight,
    final_gain,
    key_weight,
    value_weight,
    queries,
    block_lists,
    live_counts,
):
    block_rows = neighbour_rows.shape[0]
    blocks = block_rows // NB
    head_width = key_weight.shape[1]
    heads_local = head_width // DH
    row_width = 2 * head_width
    widened = neighbour_rows.astype(jnp.float32)
    normed = rms_scale(widened, norm_gain).astype(jnp.bfloat16)
    hidden = jax.nn.gelu(jnp.dot(normed, up_weight, preferred_element_type=jnp.float32)).astype(
        jnp.bfloat16
    )
    partial_sum = jnp.dot(hidden, down_weight, preferred_element_type=jnp.float32)
    encoded = widened + lax.psum(partial_sum, ("tensor", "enc"))
    final_rows = rms_scale(encoded, final_gain).astype(jnp.bfloat16)
    key_part = jnp.dot(final_rows, key_weight, preferred_element_type=jnp.float32).astype(
        jnp.bfloat16
    )
    value_part = jnp.dot(final_rows, value_weight, preferred_element_type=jnp.float32).astype(
        jnp.bfloat16
    )
    stacked = jnp.concatenate([key_part, value_part], axis=-1)
    kv_blocks = stacked.reshape(blocks, NB, row_width)
    seq_count = lax.axis_size("seq")
    span_count = live_counts.shape[0]
    need_count = span_count * KMAX
    capacity = (need_count + seq_count - 1) // seq_count
    flat_lists = block_lists.reshape(need_count)
    owners = flat_lists // blocks
    rank_order = need_ranks(owners)
    slot_index = owners * capacity + rank_order
    live_mask = jnp.arange(KMAX)[None, :] < live_counts[:, None]
    slot_range = jnp.arange(capacity)
    every_list = lax.all_gather(block_lists, "seq", axis=0, tiled=True)
    every_flat = every_list.reshape(seq_count, need_count)
    every_owner = every_flat // blocks
    every_rank = need_ranks(every_owner)
    position = lax.axis_index("seq")
    slot_match = jnp.logical_and(
        every_owner[:, :, None] == position, every_rank[:, :, None] == slot_range[None, None, :]
    )
    local_index = every_flat % blocks
    picked = jnp.sum(jnp.where(slot_match, local_index[:, :, None], 0), axis=1)
    filled = jnp.any(slot_match, axis=1)
    outgoing = jnp.take(kv_blocks, picked.reshape(-1), axis=0).reshape(
        seq_count, capacity, NB, row_width
    )
    outgoing = jnp.where(filled[:, :, None, None], outgoing, jnp.zeros((), jnp.bfloat16))
    incoming = lax.all_to_all(outgoing, "seq", split_axis=0, concat_axis=0, tiled=True)
    chosen = jnp.take(incoming.reshape(seq_count * capacity, NB, row_width), slot_index, axis=0)
    chosen = chosen.reshape(span_count, KMAX * NB, row_width)
    key_tiles = chosen[..., :head_width].reshape(span_count, KMAX * NB, heads_local, DH)
    value_tiles = chosen[..., head_width:].reshape(span_count, KMAX * NB, heads_local, DH)
    query_tiles = queries.reshape(span_count, CL, heads_local, DH)
    scores = jnp.einsum(
        "cqhd,ckhd->chqk", query_tiles, key_tiles, preferred_element_type=jnp.float32
    ) / math.sqrt(DH)
    key_mask = jnp.repeat(live_mask, NB, axis=1)
    scores = jnp.where(key_mask[:, None, None, :], scores, -1e30)
    highest = jnp.max(scores, axis=-1, keepdims=True)
    weights = jnp.exp(scores - highest)
    row_total = jnp.sum(weights, axis=-1)
    summed = jnp.einsum(
        "chqk,ckhd->cqhd",
        weights.astype(jnp.bfloat16),
        value_tiles,
        preferred_element_type=jnp.float32,
    )
    result = summed / jnp.transpose(row_total, (0, 2, 1))[..., None]
    return result.reshape(span_count * CL, head_width).astype(jnp.bfloat16)


def solution(mesh):
    placed = (
        P("seq", None),
        P(),
        P(None, ("tensor", "enc")),
        P(("tensor", "enc"), None),
        P(),
        P(None, ("tensor", "enc")),
        P(None, ("tensor", "enc")),
        P("seq", ("tensor", "enc")),
        P("seq", None),
        P("seq"),
    )
    return jax.shard_map(
        shards, mesh=mesh, in_specs=placed, out_specs=P("seq", ("tensor", "enc")), check_vma=False
    )
```

profile of v0, /device:TPU:1, one launch (start us, length us, event | category | flops | bytes accessed | tf_op | source)
XLA Modules:
  0.0 551.1 jit_solution(868867025787064083)
XLA Ops:
  6.5 2.2 fusion
  8.9 5.3 fusion.27
  14.3 0.7 copy-done.4
  14.9 116.7 %all-gather = s32[32,16,2]{1,2,0:T(2,128)S(1)} all-gather(s32[1,16,2]{1,2,0:T(2,128)S(1)} %bitcast.78), channel_id=1, replica_groups=mesh['seq'=32,'tensor'=8,'enc'=2] {'seq'}, dimensions={0}, use_global_device_ids=true | all-gather | bytes 4224 | tf_op jit(solution)/shard_map/all_gather | solution.py:70
  131.9 0.8 convert_reduce_fusion
  133.6 175.5 %all-reduce.2.cloned.1.call-done = f32[1024,1024]{1,0:T(8,128)} async-done(((f32[1024,1024]{1,0:T(8,128)}), f32[1024,1024]{1,0:T(8,128)}) %all-reduce.2.cloned.1.call-update) | async-done | bytes 4194320 | tf_op jit(solution)/shard_map/psum | solution.py:50
  309.1 2.9 multiply_reduce_fusion
  312.1 0.5 copy-done.2
  312.5 0.7 multiply_convert_fusion
  313.6 0.8 convolution_convert_fusion
  314.6 0.8 convolution_convert_fusion.1
  315.5 0.5 copy.95
  316.0 2.8 gather_fusion
  318.8 4.7 fusion.4
  323.5 18.8 %all-to-all-start = ((bf16[32,1,128,512]{3,2,1,0:T(8,128)(2,1)}), bf16[32,1,128,512]{3,2,1,0:T(8,128)(2,1)}, u32[]{:S(2)}, u32[]{:S(2)}) async-start(bf16[32,1,128,512]{3,2,1,0:T(8,128)(2,1)} %fusion.4), calls=%async_computation | async-start | bytes 8388608 | tf_op jit(solution)/shard_map/all_to_all | solution.py:85
  343.5 182.1 %all-to-all-done = bf16[32,1,128,512]{3,2,1,0:T(8,128)(2,1)} async-done(((bf16[32,1,128,512]{3,2,1,0:T(8,128)(2,1)}), bf16[32,1,128,512]{3,2,1,0:T(8,128)(2,1)}, u32[]{:S(2)}, u32[]{:S(2)}) %all-to-all-start) | async-done | bytes 4194336 | tf_op jit(solution)/shard_map/all_to_all | solution.py:85
  525.6 5.0 gather_fusion.1
  530.6 6.4 %copy.88 = bf16[16,256,512]{1,2,0:T(8,128)(2,1)} copy(bf16[16,256,512]{2,1,0:T(8,128)(2,1)} %bitcast.66) | data formatting | bytes 8388608 | tf_op jit(solution)/shard_map/jit(_take)/gather | solution.py:86
  536.9 2.6 broadcast_select_fusion
  540.0 0.7 bitcast_reduce_fusion
  540.6 1.0 fusion.10
  541.6 1.2 fusion.13
  542.8 0.5 copy.92
  543.4 0.9 copy.106
  (59 shorter events, 3.5 us)
Async XLA Ops:
  6.5 2.2 copy-start
  6.5 2.4 copy-start.1
  6.5 2.4 copy-start.9
  6.5 302.5 %all-reduce.2.cloned.1.call-start = ((), (), s32[]{:S(2)}) async-start(), calls=%async_computation.1 | async-start | bytes 8388608 | tf_op jit(solution)/shard_map/psum | solution.py:50
  14.2 0.7 copy-start.4
  133.6 178.5 %copy-start.5 = (f32[1024]{0:T(1024)S(1)}, f32[1024]{0:T(1024)}, u32[]{:S(2)}) copy-start(f32[1024]{0:T(1024)} %param.14) | copy-start | bytes 12292
  309.1 3.4 copy-start.2
  312.5 1.0 copy-start.7
  313.6 1.0 copy-start.8
  323.5 19.6 %copy-start.6 = (s32[16]{0:T(128)S(1)}, s32[16]{0:T(128)}, u32[]{:S(2)}) copy-start(s32[16]{0:T(128)} %param.19) | copy-start | bytes 196
  323.5 19.8 %copy-start.3 = (bf16[1024,256]{1,0:T(8,128)(2,1)S(1)}, bf16[1024,256]{1,0:T(8,128)(2,1)}, u32[]{:S(2)}) copy-start(bf16[1024,256]{1,0:T(8,128)(2,1)} %param.17) | copy-start | bytes 1572868
  323.5 202.1 %all-to-all-start = ((bf16[32,1,128,512]{3,2,1,0:T(8,128)(2,1)}), bf16[32,1,128,512]{3,2,1,0:T(8,128)(2,1)}, u32[]{:S(2)}, u32[]{:S(2)}) async-start(bf16[32,1,128,512]{3,2,1,0:T(8,128)(2,1)} %fusion.4), calls=%async_computation | async-start | bytes 8388608 | tf_op jit(solution)/shard_map/all_to_all | solution.py:85
Sparse Core Ops, SparseCore 0:
  14.4 294.6 all-reduce.1
where the time goes:
time: 553 us; the launch traced here: 551 us
  waiting for transfers between devices  358 us (65%)
  blocking collectives  117 us (21%)
  local copies, waits for them, and re-layouts  20 us (4%)
  starting transfers between devices  18.8 us (3%)
  other arithmetic  15.7 us (3%)
  between operations  13.7 us (2%)
  matrix products  8.7 us (2%)
    all_to_all x1, waiting for transfers between devices, shards(): lax.all_to_all(outgoing, 'seq', split_axis=0, concat_axis=0, tiled=True)  182 us
    psum x1, waiting for transfers between devices, shards(): encoded = widened + lax.psum(partial_sum, ('tensor', 'enc'))  175 us
    all_gather x1, blocking collectives, shards(): every_list = lax.all_gather(block_lists, 'seq', axis=0, tiled=True)  117 us
    all_to_all x1, starting transfers between devices, shards(): lax.all_to_all(outgoing, 'seq', split_axis=0, concat_axis=0, tiled=True)  18.8 us
    gather x2, local copies, waits for them, and re-layouts, shards(): jnp.take(incoming.reshape(seq_count * capacity, NB, row_width), slot_inde...  11.4 us
  transfers between devices with their start and end apart: 2, of which 2 were waited for; matrix products, arithmetic and copies ran while one was open for 1% of the time, Pallas kernels for 0%

commit v1 on v0

v1 whole, which is shorter than its diff:
```python
import math

import jax
import jax.numpy as jnp
from jax import lax
from jax.sharding import PartitionSpec as P

DH = 128
NB = 128
CL = 64
KMAX = 2
TAG = 128


def rms_scale(rows, gain):
    mean_square = jnp.mean(rows * rows, axis=-1, keepdims=True)
    return rows * lax.rsqrt(mean_square + 1e-06) * gain


def need_ranks(owners):
    need_count = owners.shape[-1]
    order_index = jnp.arange(need_count)
    same_owner = owners[..., :, None] == owners[..., None, :]
    earlier = order_index[None, :] < order_index[:, None]
    return jnp.sum(jnp.logical_and(same_owner, earlier), axis=-1)


def shards(
    neighbour_rows,
    norm_gain,
    up_weight,
    down_weight,
    final_gain,
    key_weight,
    value_weight,
    queries,
    block_lists,
    live_counts,
):
    block_rows = neighbour_rows.shape[0]
    blocks = block_rows // NB
    head_width = key_weight.shape[1]
    heads_local = head_width // DH
    seq_count = lax.axis_size("seq")
    span_count = live_counts.shape[0]
    need_count = span_count * KMAX
    capacity = (need_count + seq_count - 1) // seq_count
    slots = seq_count * capacity
    q_width = CL * head_width

    flat_lists = block_lists.reshape(need_count)
    owners = flat_lists // blocks
    rank_order = need_ranks(owners)
    slot_index = owners * capacity + rank_order
    slot_range = jnp.arange(slots)
    slot_match = slot_index[None, :] == slot_range[:, None]
    entry_of_slot = jnp.sum(jnp.where(slot_match, jnp.arange(need_count)[None, :], 0), axis=1)
    filled = jnp.any(slot_match, axis=1)
    span_of_slot = entry_of_slot // KMAX
    block_of_slot = jnp.where(filled, flat_lists[entry_of_slot] % blocks, 0)
    span_queries = queries.reshape(span_count, q_width)
    sent_queries = jnp.take(span_queries, span_of_slot, axis=0)
    sent_queries = jnp.where(filled[:, None], sent_queries, jnp.zeros((), jnp.bfloat16))
    tag = jnp.broadcast_to(block_of_slot.astype(jnp.bfloat16)[:, None], (slots, TAG))
    outgoing = jnp.concatenate([sent_queries, tag], axis=1)
    incoming = lax.all_to_all(outgoing, "seq", split_axis=0, concat_axis=0, tiled=True)

    widened = neighbour_rows.astype(jnp.float32)
    normed = rms_scale(widened, norm_gain).astype(jnp.bfloat16)
    hidden = jax.nn.gelu(jnp.dot(normed, up_weight, preferred_element_type=jnp.float32)).astype(
        jnp.bfloat16
    )
    partial_sum = jnp.dot(hidden, down_weight, preferred_element_type=jnp.float32)
    reduced = lax.psum_scatter(partial_sum, ("tensor", "enc"), scatter_dimension=0, tiled=True)
    piece_rows = reduced.shape[0]
    piece = lax.axis_index("tensor") * lax.axis_size("enc") + lax.axis_index("enc")
    own_rows = lax.dynamic_slice_in_dim(neighbour_rows, piece * piece_rows, piece_rows, axis=0)
    encoded = own_rows.astype(jnp.float32) + reduced
    final_piece = rms_scale(encoded, final_gain).astype(jnp.bfloat16)
    final_rows = lax.all_gather(final_piece, ("tensor", "enc"), axis=0, tiled=True)
    key_part = jnp.dot(final_rows, key_weight, preferred_element_type=jnp.float32).astype(
        jnp.bfloat16
    )
    value_part = jnp.dot(final_rows, value_weight, preferred_element_type=jnp.float32).astype(
        jnp.bfloat16
    )
    key_blocks = key_part.reshape(blocks, NB, heads_local, DH)
    value_blocks = value_part.reshape(blocks, NB, heads_local, DH)

    in_queries = incoming[:, :q_width].reshape(slots, CL, heads_local, DH)
    in_block = incoming[:, q_width].astype(jnp.int32)
    in_block = jnp.clip(in_block, 0, blocks - 1)
    key_tiles = jnp.take(key_blocks, in_block, axis=0)
    value_tiles = jnp.take(value_blocks, in_block, axis=0)
    scores = jnp.einsum(
        "sqhd,skhd->shqk", in_queries, key_tiles, preferred_element_type=jnp.float32
    ) / math.sqrt(DH)
    local_max = jnp.max(scores, axis=-1, keepdims=True)
    weights = jnp.exp(scores - local_max)
    local_total = jnp.sum(weights, axis=-1)
    summed = jnp.einsum(
        "shqk,skhd->sqhd",
        weights.astype(jnp.bfloat16),
        value_tiles,
        preferred_element_type=jnp.float32,
    )
    stats = jnp.concatenate(
        [local_max[..., 0].reshape(slots, -1), local_total.reshape(slots, -1)], axis=1
    )
    reply = jnp.concatenate([summed.reshape(slots, q_width), stats], axis=1)
    returned = lax.all_to_all(reply, "seq", split_axis=0, concat_axis=0, tiled=True)

    stat_width = heads_local * CL
    picked = jnp.take(returned, slot_index, axis=0).reshape(span_count, KMAX, -1)
    part_sum = picked[..., :q_width].reshape(span_count, KMAX, CL, heads_local, DH)
    part_max = picked[..., q_width : q_width + stat_width].reshape(
        span_count, KMAX, heads_local, CL
    )
    part_total = picked[..., q_width + stat_width :].reshape(span_count, KMAX, heads_local, CL)
    live_mask = (jnp.arange(KMAX)[None, :] < live_counts[:, None])[:, :, None, None]
    part_max = jnp.where(live_mask, part_max, -jnp.inf)
    highest = jnp.max(part_max, axis=1, keepdims=True)
    scale = jnp.where(live_mask, jnp.exp(part_max - highest), 0.0)
    row_total = jnp.sum(scale * part_total, axis=1)
    scale_rows = jnp.transpose(scale, (0, 1, 3, 2))[..., None]
    combined = jnp.sum(jnp.where(scale_rows > 0, scale_rows * part_sum, 0.0), axis=1)
    result = combined / jnp.transpose(row_total, (0, 2, 1))[..., None]
    return result.reshape(span_count * CL, head_width).astype(jnp.bfloat16)


def solution(mesh):
    placed = (
        P("seq", None),
        P(),
        P(None, ("tensor", "enc")),
        P(("tensor", "enc"), None),
        P(),
        P(None, ("tensor", "enc")),
        P(None, ("tensor", "enc")),
        P("seq", ("tensor", "enc")),
        P("seq", None),
        P("seq"),
    )
    return jax.shard_map(
        shards, mesh=mesh, in_specs=placed, out_specs=P("seq", ("tensor", "enc")), check_vma=False
    )
```

time: 553 us -> 444 us (0.80)
  blocking collectives: 117 us -> 0 us
  waiting for transfers between devices: 358 us -> 308 us
  local copies, waits for them, and re-layouts: 20 us -> 68 us
  matrix products: 8.7 us -> 15.8 us
    all_to_all x1, waiting for transfers between devices: 182 us -> 0.01 us  [shards(): lax.all_to_all(outgoing, 'seq', split_axis=0, concat_axis=0, tiled=True)]
    psum x1 -> x0, waiting for transfers between devices: 175 us -> none  [shards(): encoded = widened + lax.psum(partial_sum, ('tensor', 'enc'))]
    reduce_scatter x0 -> x1, waiting for transfers between devices: none -> 146 us  [shards(): lax.psum_scatter(partial_sum, ('tensor', 'enc'), scatter_dimension=0, til...]
    all_gather x1 -> x0, blocking collectives: 117 us -> none  [shards(): every_list = lax.all_gather(block_lists, 'seq', axis=0, tiled=True)]
    all_to_all x0 -> x1, waiting for transfers between devices: none -> 96.1 us  [shards(): lax.all_to_all(reply, 'seq', split_axis=0, concat_axis=0, tiled=True)]
    all_gather x0 -> x1, waiting for transfers between devices: none -> 65.9 us  [shards(): lax.all_gather(final_piece, ('tensor', 'enc'), axis=0, tiled=True)]
    all_to_all x0 -> x3, local copies, waits for them, and re-layouts: none -> 9.29 us  [the longest x2 5.78 us: shards(): lax.all_to_all(outgoing, 'seq', split_axis=0, concat_axis=0, tiled=True)]
    mul x0 -> x2, local copies, waits for them, and re-layouts: none -> 8.66 us  [shards(): scale_rows * part_sum]
  transfers between devices with their start and end apart: 2 -> 4, of which waited for: 2 -> 3; matrix products, arithmetic and copies ran while one was open for 1% -> 7% of each run, Pallas kernels for 0% -> 0%
where the time goes in v1:
time: 444 us; the launch traced here: 443 us
  waiting for transfers between devices  308 us (69%)
  local copies, waits for them, and re-layouts  68 us (15%)
  starting transfers between devices  21.7 us (5%)
  matrix products  15.8 us (4%)
  other arithmetic  15.6 us (4%)
  between operations  13.8 us (3%)
    reduce_scatter x1, waiting for transfers between devices, shards(): lax.psum_scatter(partial_sum, ('tensor', 'enc'), scatter_dimension=0, til...  146 us
    all_to_all x1, waiting for transfers between devices, shards(): lax.all_to_all(reply, 'seq', split_axis=0, concat_axis=0, tiled=True)  96.1 us
    all_gather x1, waiting for transfers between devices, shards(): lax.all_gather(final_piece, ('tensor', 'enc'), axis=0, tiled=True)  65.9 us
    all_to_all x1, starting transfers between devices, shards(): lax.all_to_all(outgoing, 'seq', split_axis=0, concat_axis=0, tiled=True)  16.2 us
    unnamed x24, local copies, waits for them, and re-layouts  9.49 us
  transfers between devices with their start and end apart: 4, of which 3 were waited for; matrix products, arithmetic and copies ran while one was open for 7% of the time, Pallas kernels for 0%

profile of v1, /device:TPU:1, one launch (start us, length us, event | category | flops | bytes accessed | tf_op | source)
XLA Modules:
  0.0 442.7 jit_solution(8348694677223937590)
XLA Ops:
  8.9 5.3 %fusion.33 = f32[1024,1024]{1,0:T(8,128)} fusion(bf16[256,1024]{1,0:T(8,128)(2,1)S(1)} %copy-done, bf16[1024,256]{1,0:T(8,128)(2,1)} %param.14, bf16[1024,1024]{1,0:T(8,128)(2,1)S(1)} %copy-done.2, f32[1024]{0:T(1024)S(1)} %copy-done.8, f32[1024]{0:T(1024)S(1)} %add_rsqrt_fusion), kind=kOutput, calls=%fused_computation.42 | convolution fusion | flops 1080295424 | bytes 7348224 | tf_op jit(solution)/shard_map/dot_general | solution.py:73
  21.7 16.2 %all-to-all-start = ((bf16[32,2,8256]{2,1,0:T(2,128)(2,1)}), bf16[32,2,8256]{2,1,0:T(2,128)(2,1)}, u32[]{:S(2)}, u32[]{:S(2)}) async-start(bf16[32,2,8256]{2,1,0:T(2,128)(2,1)} %reshape.393), calls=%async_computation.1 | async-start | bytes 2129920 | tf_op jit(solution)/shard_map/all_to_all | solution.py:66
  38.1 145.8 %reduce-scatter.2.cloned.1.call-done = f32[64,1024]{1,0:T(8,128)} async-done(((f32[1024,1024]{1,0:T(8,128)}), f32[64,1024]{1,0:T(8,128)}) %reduce-scatter.2.cloned.1.call-update) | async-done | bytes 262160 | tf_op jit(solution)/shard_map/reduce_scatter | solution.py:74
  186.8 4.4 %reshape.394 = bf16[32,1,16512]{2,1,0:T(2,128)(2,1)S(1)} reshape(bf16[32,2,8256]{2,1,0:T(2,128)(2,1)} %all-to-all-done) | data formatting | bytes 2113536
  191.2 5.3 %copy.112 = bf16[32,1,16512]{0,2,1:T(8,128)(2,1)} copy(bf16[32,1,16512]{2,1,0:T(2,128)(2,1)S(1)} %reshape.394) | data formatting | bytes 2113536 | tf_op jit(solution)/shard_map/all_to_all | solution.py:66
  196.5 3.8 slice.30
  200.3 4.9 %copy.116 = bf16[32,64,2,128]{3,1,2,0:T(8,128)(2,1)} copy(bf16[32,64,2,128]{0,3,2,1:T(8,128)(2,1)} %bitcast.63) | data formatting | bytes 2097152 | tf_op jit(solution)/shard_map/reshape | solution.py:90
  205.9 65.9 %all-gather.2.cloned.1.call-done = bf16[1024,1024]{1,0:T(8,128)(2,1)} async-done(((bf16[64,1024]{1,0:T(8,128)(2,1)}), bf16[1024,1024]{1,0:T(8,128)(2,1)}) %all-gather.2.cloned.1.call-update) | async-done | bytes 2097168 | tf_op jit(solution)/shard_map/all_gather | solution.py:80
  271.8 2.3 convolution_convert_fusion.1
  275.1 2.3 convolution_convert_fusion
  279.9 3.6 multiply_reduce_fusion
  287.2 2.4 fusion.17
  289.5 3.0 copy.117
  292.5 2.9 reshape.343
  295.6 3.5 copy.118
  299.1 5.3 %all-to-all-start.1 = ((f32[32,1,16640]{2,1,0:T(1,128)}), f32[32,1,16640]{2,1,0:T(1,128)}, u32[]{:S(2)}, u32[]{:S(2)}) async-start(f32[32,1,16640]{2,1,0:T(1,128)} %copy.118), calls=%async_computation.2 | async-start | bytes 4259840 | tf_op jit(solution)/shard_map/all_to_all | solution.py:111
  304.8 96.1 %all-to-all-done.1 = f32[32,1,16640]{2,1,0:T(1,128)} async-done(((f32[32,1,16640]{2,1,0:T(1,128)}), f32[32,1,16640]{2,1,0:T(1,128)}, u32[]{:S(2)}, u32[]{:S(2)}) %all-to-all-start.1) | async-done | bytes 2129952 | tf_op jit(solution)/shard_map/all_to_all | solution.py:111
  402.7 2.5 gather_fusion.2
  405.2 3.5 gather.19
  411.8 4.3 broadcast_in_dim.130
  416.1 3.0 broadcast_in_dim.131
  420.5 4.8 %mul.99 = f32[16,2,64,2,128]{4,3,2,0,1:T(2,128)} broadcast(f32[16,2,64,2]{3,2,0,1:T(8,128)} %copy.124), dimensions={0,1,2,3} | broadcast | bytes 2113536 | tf_op jit(solution)/shard_map/mul | solution.py:126
  425.3 3.9 mul.100
  429.2 3.0 fusion.6
  (84 shorter events, 30.9 us)
Async XLA Ops:
  6.5 2.2 copy-start
  6.5 2.4 copy-start.2
  6.5 2.4 copy-start.8
  6.5 177.3 %reduce-scatter.2.cloned.1.call-start = ((), (), s32[]{:S(2)}) async-start(), calls=%async_computation.3 | async-start | bytes 4456448 | tf_op jit(solution)/shard_map/reduce_scatter | solution.py:74
  14.2 0.7 copy-start.5
  14.2 1.9 copy-start.3
  20.0 165.0 %copy-start.4 = (f32[1024]{0:T(1024)S(1)}, f32[1024]{0:T(1024)}, u32[]{:S(2)}) copy-start(f32[1024]{0:T(1024)} %param.16) | copy-start | bytes 12292
  21.7 165.1 %all-to-all-start = ((bf16[32,2,8256]{2,1,0:T(2,128)(2,1)}), bf16[32,2,8256]{2,1,0:T(2,128)(2,1)}, u32[]{:S(2)}, u32[]{:S(2)}) async-start(bf16[32,2,8256]{2,1,0:T(2,128)(2,1)} %reshape.393), calls=%async_computation.1 | async-start | bytes 2129920 | tf_op jit(solution)/shard_map/all_to_all | solution.py:66
  37.9 233.9 %all-gather.2.cloned.1.call-start = ((), (), s32[]{:S(2)}) async-start(), calls=%async_computation.4 | async-start | bytes 2228224 | tf_op jit(solution)/shard_map/all_gather | solution.py:80
  200.3 71.5 %copy-start.6 = (bf16[1024,256]{1,0:T(8,128)(2,1)S(1)}, bf16[1024,256]{1,0:T(8,128)(2,1)}, u32[]{:S(2)}) copy-start(bf16[1024,256]{1,0:T(8,128)(2,1)} %param.18) | copy-start | bytes 1572868
  274.1 1.0 copy-start.7
  299.1 5.6 %copy-start.9 = (s32[16]{0:T(128)S(1)}, s32[16]{0:T(128)}, u32[]{:S(2)}) copy-start(s32[16]{0:T(128)} %param.21) | copy-start | bytes 196
  299.1 101.8 %all-to-all-start.1 = ((f32[32,1,16640]{2,1,0:T(1,128)}), f32[32,1,16640]{2,1,0:T(1,128)}, u32[]{:S(2)}, u32[]{:S(2)}) async-start(f32[32,1,16640]{2,1,0:T(1,128)} %copy.118), calls=%async_computation.2 | async-start | bytes 4259840 | tf_op jit(solution)/shard_map/all_to_all | solution.py:111
  432.2 3.6 copy-start.1
Sparse Core Ops, SparseCore 0:
  14.3 169.5 reduce-scatter.1
  187.2 84.5 all-gather.1
